TPU v7x, 32 devices: a whole 2x2x4 slice. The times are simulated.
32 devices in a mesh: dp: 4 (over z), ctx: 8 (over y, x, core).
Axes of the slice: x: 2, y: 2, z: 4, core: 2. Of those that a mesh axis runs over, the one named last changes fastest.
Arguments:
- tokens: bfloat16 [4, 1024, 6144], P('dp', 'ctx'), may hold values from -0.1875 to 0.1875
- cotangent: bfloat16 [4, 1024, 6144], P('dp', 'ctx'), may hold values from -6 to 6
- w_router: float32 [6144], replicated, may hold values from -2 to 2
- w_query: bfloat16 [6144, 4096], P(None, 'ctx'), may hold values from -0.078125 to 0.078125
- w_key: bfloat16 [6144, 4096], P(None, 'ctx'), may hold values from -0.078125 to 0.078125
- w_value: bfloat16 [6144, 4096], P(None, 'ctx'), may hold values from -0.078125 to 0.078125
- w_out: bfloat16 [4096, 6144], P('ctx'), may hold values from -0.09375 to 0.09375
- chosen: int32 [4, 160], P('dp', 'ctx'), may hold values from -1 to 1023, as said below
- counts: int32 [4, 8], P('dp', 'ctx'), may hold values from 12 to 20, as said below
Outputs:
- layer_out: bfloat16 [4, 1024, 6144], P('dp', 'ctx')
- grad_query: bfloat16 [6144, 4096], P('dp', 'ctx')
- grad_key: bfloat16 [6144, 4096], P('dp', 'ctx')
- grad_value: bfloat16 [6144, 4096], P('dp', 'ctx')
- grad_out: bfloat16 [4096, 6144], P('ctx', 'dp')
- grad_router: float32 [6144], replicated
Inputs may be any that keep to these rules, and one draw needn't show every extreme that they name: `chosen`: for every sequence b and device block c, the first counts[b, c] of the block's slots c * 20 to (c + 1) * 20 - 1 hold increasing positions of that device's tokens, c * 128 to (c + 1) * 128 - 1; the other slots hold -1. In every sequence the counts add up to 128, and some device's block has exactly 20 used slots.
All inputs are finite; a program needn't handle non-finite values.
Results may differ from a plain program's by a relative error of at most 0.018.
Values may be sent and summed in bfloat16 or wider, within the bound.
No kernel may reach another device: no remote copies, remote signals or barrier semaphores. Data moves between devices by JAX's collectives and lax.ppermute only.
A program may use at most 128 MiB of HBM per device.

v0:
```python
import math
import jax
import jax.numpy as jnp
from jax import lax
from jax.sharding import PartitionSpec as P

HDIM = 128
HIGHEST_PRECISION = lax.Precision.HIGHEST
ROW_CONTRACT = (((0,), (0,)), ((), ()))
COLUMN_CONTRACT = (((1,), (1,)), ((), ()))


def head_norm(values, width):
    shaped = values.reshape(values.shape[0], -1, width)
    inverse = lax.rsqrt(jnp.mean(shaped * shaped, axis=-1, keepdims=True) + 1e-06)
    return (shaped * inverse, inverse)


def norm_back(grad_hat, normal, inverse):
    return inverse * (grad_hat - normal * jnp.mean(grad_hat * normal, axis=-1, keepdims=True))


def rounded_term(part):
    return lax.optimization_barrier(part.astype(jnp.bfloat16)).astype(jnp.float32)


def body(tokens, cotangent, w_router, w_query, w_key, w_value, w_out, chosen, counts):
    length = tokens.shape[1]
    capacity = chosen.shape[1]
    inner = w_query.shape[1]
    heads_here = inner // HDIM
    scale = 1.0 / math.sqrt(HDIM)
    offset = lax.axis_index("ctx") * length
    slot_ids = lax.broadcasted_iota(jnp.int32, (capacity,), 0)
    local = chosen[0] - offset
    present = (slot_ids < counts[0, 0]) & (local >= 0) & (local < length)
    columns = lax.broadcasted_iota(jnp.int32, (capacity, length), 1)
    onehot = ((local[:, None] == columns) & present[:, None]).astype(jnp.bfloat16)
    rows = jnp.dot(onehot, tokens[0], preferred_element_type=jnp.float32)
    rows_back = jnp.dot(onehot, cotangent[0], preferred_element_type=jnp.float32)
    logits = jnp.dot(rows, w_router, precision=HIGHEST_PRECISION)
    weights = jax.nn.sigmoid(logits)
    normed = (rows * lax.rsqrt(jnp.mean(rows * rows, axis=-1, keepdims=True) + 1e-05)).astype(
        jnp.bfloat16
    )
    delta = (weights[:, None] * rows_back).astype(jnp.bfloat16)
    all_normed, all_delta, all_present = (
        lax.all_gather(normed, "ctx", axis=0, tiled=True),
        lax.all_gather(delta, "ctx", axis=0, tiled=True),
        lax.all_gather(present.astype(jnp.bfloat16), "ctx", axis=0, tiled=True),
    )
    slots = all_normed.shape[0]
    query_raw = jnp.dot(all_normed, w_query, preferred_element_type=jnp.float32)
    key_raw = jnp.dot(all_normed, w_key, preferred_element_type=jnp.float32)
    value_raw = jnp.dot(all_normed, w_value, preferred_element_type=jnp.float32)
    query_hat, query_scale = head_norm(query_raw, HDIM)
    key_hat, key_scale = head_norm(key_raw, HDIM)
    query_b = query_hat.astype(jnp.bfloat16)
    key_b = key_hat.astype(jnp.bfloat16)
    value_b = value_raw.reshape(slots, heads_here, HDIM).astype(jnp.bfloat16)
    current = lax.broadcasted_iota(jnp.int32, (slots, slots), 0)
    earlier = lax.broadcasted_iota(jnp.int32, (slots, slots), 1)
    allowed = (earlier <= current) & ((all_present[None, :] > 0.5) | (earlier == current))
    scores = jnp.einsum("ihd,jhd->hij", query_b, key_b, preferred_element_type=jnp.float32) * scale
    exponent = jnp.where(allowed[None], jnp.exp(scores), 0.0)
    attend = exponent / jnp.sum(exponent, axis=-1, keepdims=True)
    attend_b = attend.astype(jnp.bfloat16)
    mixed = jnp.einsum("hij,jhd->ihd", attend_b, value_b, preferred_element_type=jnp.float32)
    mixed = mixed.astype(jnp.bfloat16).reshape(slots, inner)
    update = lax.psum_scatter(
        rounded_term(jnp.dot(mixed, w_out, preferred_element_type=jnp.float32)).astype(
            jnp.bfloat16
        ),
        "ctx",
        scatter_dimension=0,
        tiled=True,
    ).astype(jnp.float32)
    scaled = weights[:, None] * update
    spread = jnp.dot(onehot.astype(jnp.float32).T, scaled, precision=HIGHEST_PRECISION)
    layer_out = (tokens[0].astype(jnp.float32) + spread).astype(jnp.bfloat16)[None]
    gate_back = jnp.sum(rows_back * update, axis=-1) * weights * (1.0 - weights)
    router_part = jnp.dot(gate_back, rows, precision=HIGHEST_PRECISION)
    grad_router = lax.psum(router_part, ("dp", "ctx"))
    out_term = rounded_term(
        lax.dot_general(mixed, all_delta, ROW_CONTRACT, preferred_element_type=jnp.float32)
    )
    mixed_back = lax.dot_general(
        all_delta, w_out, COLUMN_CONTRACT, preferred_element_type=jnp.float32
    )
    mixed_back = mixed_back.astype(jnp.bfloat16).reshape(slots, heads_here, HDIM)
    attend_back = jnp.einsum(
        "ihd,jhd->hij", mixed_back, value_b, preferred_element_type=jnp.float32
    )
    inner_sum = jnp.sum(attend * attend_back, axis=-1, keepdims=True)
    scores_back = (attend * (attend_back - inner_sum) * scale).astype(jnp.bfloat16)
    value_back = jnp.einsum(
        "hij,ihd->jhd", attend_b, mixed_back, preferred_element_type=jnp.float32
    )
    value_back = value_back.astype(jnp.bfloat16).reshape(slots, inner)
    qhat_back = jnp.einsum("hij,jhd->ihd", scores_back, key_b, preferred_element_type=jnp.float32)
    khat_back = jnp.einsum("hij,ihd->jhd", scores_back, query_b, preferred_element_type=jnp.float32)
    query_back = (
        norm_back(qhat_back, query_hat, query_scale).astype(jnp.bfloat16).reshape(slots, inner)
    )
    key_back = norm_back(khat_back, key_hat, key_scale).astype(jnp.bfloat16).reshape(slots, inner)
    query_term = rounded_term(
        lax.dot_general(all_normed, query_back, ROW_CONTRACT, preferred_element_type=jnp.float32)
    )
    key_term = rounded_term(
        lax.dot_general(all_normed, key_back, ROW_CONTRACT, preferred_element_type=jnp.float32)
    )
    value_term = rounded_term(
        lax.dot_general(all_normed, value_back, ROW_CONTRACT, preferred_element_type=jnp.float32)
    )
    grad_query, grad_key, grad_value, grad_out = (
        lax.psum_scatter(
            query_term.astype(jnp.bfloat16), "dp", scatter_dimension=0, tiled=True
        ).astype(jnp.float32),
        lax.psum_scatter(
            key_term.astype(jnp.bfloat16), "dp", scatter_dimension=0, tiled=True
        ).astype(jnp.float32),
        lax.psum_scatter(
            value_term.astype(jnp.bfloat16), "dp", scatter_dimension=0, tiled=True
        ).astype(jnp.float32),
        lax.psum_scatter(
            out_term.astype(jnp.bfloat16), "dp", scatter_dimension=1, tiled=True
        ).astype(jnp.float32),
    )
    return (
        layer_out,
        grad_query.astype(jnp.bfloat16),
        grad_key.astype(jnp.bfloat16),
        grad_value.astype(jnp.bfloat16),
        grad_out.astype(jnp.bfloat16),
        grad_router,
    )


def solution(mesh):
    in_specs = (
        P("dp", "ctx", None),
        P("dp", "ctx", None),
        P(),
        P(None, "ctx"),
        P(None, "ctx"),
        P(None, "ctx"),
        P("ctx", None),
        P("dp", "ctx"),
        P("dp", "ctx"),
    )
    out_specs = (
        P("dp", "ctx", None),
        P("dp", "ctx"),
        P("dp", "ctx"),
        P("dp", "ctx"),
        P("ctx", "dp"),
        P(),
    )
    return jax.shard_map(body, mesh=mesh, in_specs=in_specs, out_specs=out_specs, check_vma=False)
```

profile of v0, /device:TPU:0, one launch (start us, length us, event | category | flops | bytes accessed | tf_op | source)
XLA Modules:
  0.0 630.2 jit_solution(3186163892697100419)
XLA Ops:
  8.0 0.7 fusion.88
  8.7 1.9 multiply_reduce_fusion.1
  10.6 0.9 fusion.31
  11.6 0.7 fusion.89
  13.1 15.3 %all-reduce = bf16[160]{0:T(256)(128)(2,1)S(1)} all-reduce(bf16[160]{0:T(256)(128)(2,1)S(1)} %dynamic-update-slice), channel_id=1, replica_groups=mesh['dp'=4,'ctx'=8] {'ctx'}, use_global_device_ids=true, to_apply=%add | all-reduce | flops 160 | bytes 640
  28.4 0.7 fusion.54
  29.2 14.3 %all-gather.5.cloned.1.call-done = bf16[8,20,6144]{2,1,0:T(8,128)(2,1)} async-done(((bf16[1,20,6144]{2,1,0:T(8,128)(2,1)}), bf16[8,20,6144]{2,1,0:T(8,128)(2,1)}) %all-gather.5.cloned.1.call-update) | async-done | bytes 1966096 | tf_op jit(solution)/shard_map/all_gather | solution.py:48
  43.4 2.6 reshape.127
  46.0 4.8 fusion.16
  50.8 4.8 fusion.103
  55.7 1.9 fusion.102
  57.6 1.8 reshape.116
  59.4 1.9 multiply_reduce_fusion.5
  61.3 1.0 copy.67
  62.2 1.8 reshape.117
  64.0 1.9 multiply_reduce_fusion.4
  65.9 1.0 copy.69
  66.9 2.4 fusion.28
  69.2 1.5 fusion.14
  70.8 0.6 copy-done.7
  71.4 5.4 convolution_convert_fusion.4
  76.8 30.2 %fusion = bf16[24,6144]{1,0:T(8,128)(2,1)} fusion(bf16[160,6144]{1,0:T(8,128)(2,1)} %convolution_convert_fusion.4), kind=kCustom, calls=%all-reduce-scatter | all-reduce-scatter fusion | flops 1179649 | bytes 2261504
  106.9 2.0 collective-permute-start
  108.9 1.5 slice
  110.5 3.2 collective-permute-start.1
  113.7 2.3 fusion.21
  116.6 9.6 %concatenate = bf16[52,6144]{1,0:T(8,128)(2,1)} concatenate(bf16[4,6144]{1,0:T(4,128)(2,1)} %collective-permute-done.1, bf16[24,6144]{1,0:T(8,128)(2,1)} %collective-permute-done, bf16[24,6144]{1,0:T(8,128)(2,1)} %fusion), dimensions={0} | concatenate | bytes 1277952
  126.2 2.8 fusion.26
  129.1 30.2 %all-gather.7.cloned.1.call-done = bf16[8,20,6144]{2,1,0:T(8,128)(2,1)} async-done(((bf16[1,20,6144]{2,1,0:T(8,128)(2,1)}), bf16[8,20,6144]{2,1,0:T(8,128)(2,1)}) %all-gather.7.cloned.1.call-update) | async-done | bytes 1966096 | tf_op jit(solution)/shard_map/all_gather | solution.py:49
  159.3 4.0 reshape.129
  163.3 6.0 convolution_convert_fusion
  169.6 5.8 fusion.17
  175.4 0.7 copy-done.10
  176.1 1.1 fusion.48
  177.2 2.6 multiply_reduce_fusion.3
  179.8 5.7 convolution_convert_fusion.3
  185.6 2.4 multiply_reduce_fusion.2
  188.0 5.6 convolution_convert_fusion.2
  193.6 0.8 copy-done.11
  194.7 4.4 convolution_convert_fusion.1
  199.2 1.0 copy-done.3
  200.2 0.4 fusion.77
  200.6 47.0 %psum.7 = f32[6144]{0:T(1024)} all-reduce(f32[6144]{0:T(1024)S(1)} %bitcast.169), channel_id=1, replica_groups=mesh['dp'=4,'ctx'=8] {'dp','ctx'}, use_global_device_ids=true, to_apply=%region_13.14 | all-reduce | flops 6144 | bytes 49152 | tf_op jit(solution)/shard_map/psum | solution.py:83
  247.6 4.4 fusion.3
  252.0 29.3 %reduce-scatter.13.cloned.1.call-done = bf16[512,1536]{1,0:T(8,128)(2,1)} async-done(((bf16[512,6144]{1,0:T(8,128)(2,1)}), bf16[512,1536]{1,0:T(8,128)(2,1)}) %reduce-scatter.13.cloned.1.call-update) | async-done | bytes 1572880 | tf_op jit(solution)/shard_map/reduce_scatter | solution.py:125
  281.3 114.0 %reduce-scatter.7.cloned.1.call-done = bf16[1536,512]{1,0:T(8,128)(2,1)} async-done(((bf16[6144,512]{1,0:T(8,128)(2,1)}), bf16[1536,512]{1,0:T(8,128)(2,1)}) %reduce-scatter.7.cloned.1.call-update) | async-done | bytes 1572880 | tf_op jit(solution)/shard_map/reduce_scatter | solution.py:116
  395.3 114.0 %reduce-scatter.9.cloned.1.call-done = bf16[1536,512]{1,0:T(8,128)(2,1)} async-done(((bf16[6144,512]{1,0:T(8,128)(2,1)}), bf16[1536,512]{1,0:T(8,128)(2,1)}) %reduce-scatter.9.cloned.1.call-update) | async-done | bytes 1572880 | tf_op jit(solution)/shard_map/reduce_scatter | solution.py:119
  509.3 114.0 %reduce-scatter.11.cloned.1.call-done = bf16[1536,512]{1,0:T(8,128)(2,1)} async-done(((bf16[6144,512]{1,0:T(8,128)(2,1)}), bf16[1536,512]{1,0:T(8,128)(2,1)}) %reduce-scatter.11.cloned.1.call-update) | async-done | bytes 1572880 | tf_op jit(solution)/shard_map/reduce_scatter | solution.py:122
  (61 shorter events, 1.1 us)
Async XLA Ops:
  7.2 119.0 %copy-start = (bf16[1,128,6144]{2,1,0:T(8,128)(2,1)S(1)}, bf16[1,128,6144]{2,1,0:T(8,128)(2,1)}, u32[]{:S(2)}) copy-start(bf16[1,128,6144]{2,1,0:T(8,128)(2,1)} %param.10) | copy-start | bytes 4718596
  7.2 4.4 copy-start.18
  7.2 36.2 %all-gather.5.cloned.1.call-start = ((), (), s32[]{:S(2)}) async-start(), calls=%async_computation.8 | async-start | bytes 2654208 | tf_op jit(solution)/shard_map/all_gather | solution.py:48
  8.7 20.5 %copy-start.12 = (pred[20]{0:T(512)(128)(4,1)}, pred[20]{0:T(512)(128)(4,1)S(1)}, u32[]{:S(2)}) copy-start(pred[20]{0:T(512)(128)(4,1)S(1)} %get-tuple-element.7) | copy-start | bytes 64
  8.7 20.5 %copy-start.14 = (s32[20]{0:T(128)}, s32[20]{0:T(128)S(1)}, u32[]{:S(2)}) copy-start(s32[20]{0:T(128)S(1)} %get-tuple-element.8) | copy-start | bytes 244
  10.6 18.6 %copy-start.2 = (f32[20,6144]{1,0:T(8,128)}, f32[20,6144]{1,0:T(8,128)S(1)}, u32[]{:S(2)}) copy-start(f32[20,6144]{1,0:T(8,128)S(1)} %get-tuple-element.14) | copy-start | bytes 1474564
  11.5 147.8 %all-gather.7.cloned.1.call-start = ((), (), s32[]{:S(2)}) async-start(), calls=%async_computation.9 | async-start | bytes 2654208 | tf_op jit(solution)/shard_map/all_gather | solution.py:49
  46.0 9.6 %slice-start = ((s8[6291456]{0:T(1024)(128)(4,1)}), s8[4194304]{0:T(1024)(128)(4,1)S(1)}, s32[]{:S(2)}) async-start(s8[6291456]{0:T(1024)(128)(4,1)} %bitcast.167), calls=%async_computation.10 | async-start | bytes 8388608
  50.8 4.8 slice-start.1
  70.7 0.7 copy-start.7
  76.8 49.5 %copy-start.13 = (pred[20]{0:T(512)(128)(4,1)S(1)}, pred[20]{0:T(512)(128)(4,1)}, u32[]{:S(2)}) copy-start(pred[20]{0:T(512)(128)(4,1)} %copy-done.12) | copy-start | bytes 64
  76.8 49.5 %copy-start.15 = (s32[20]{0:T(128)S(1)}, s32[20]{0:T(128)}, u32[]{:S(2)}) copy-start(s32[20]{0:T(128)} %copy-done.14) | copy-start | bytes 244
  106.9 9.7 %collective-permute-start = (bf16[24,6144]{1,0:T(8,128)(2,1)}, bf16[24,6144]{1,0:T(8,128)(2,1)}, u32[]{:S(2)}, u32[]{:S(2)}) collective-permute-start(bf16[24,6144]{1,0:T(8,128)(2,1)} %fusion), channel_id=1, source_target_pairs={{0,1},{1,2},{2,3},{3,4},{4,5},{5,6},{6,7},{8,9},{9,10},{10,11},{11... | collective-permute-start | bytes 884744
  110.5 6.2 collective-permute-start.1
  129.0 34.3 %copy-start.8 = (bf16[4,20,8,128]{3,2,1,0:T(8,128)(2,1)S(1)}, bf16[4,20,8,128]{3,2,1,0:T(8,128)(2,1)}, u32[]{:S(2)}) copy-start(bf16[4,20,8,128]{3,2,1,0:T(8,128)(2,1)} %copy-done.7) | copy-start | bytes 491524
  129.1 152.3 %reduce-scatter.13.cloned.1.call-start = ((), (), s32[]{:S(2)}) async-start(), calls=%async_computation.7 | async-start | bytes 7864320 | tf_op jit(solution)/shard_map/reduce_scatter | solution.py:125
  169.4 6.8 %copy-start.9 = (bf16[20,4,8,128]{3,2,1,0:T(8,128)(2,1)S(1)}, bf16[20,4,8,128]{3,2,1,0:T(8,128)(2,1)}, u32[]{:S(2)}) copy-start(bf16[20,4,8,128]{3,2,1,0:T(8,128)(2,1)} %fusion.16) | copy-start | bytes 491524
  169.4 7.8 %copy-start.4 = (f32[160,512]{1,0:T(8,128)S(1)}, f32[160,512]{1,0:T(8,128)}, u32[]{:S(2)}) copy-start(f32[160,512]{1,0:T(8,128)} %fusion.103) | copy-start | bytes 983044
  169.4 7.8 %copy-start.5 = (f32[160,512]{1,0:T(8,128)S(1)}, f32[160,512]{1,0:T(8,128)}, u32[]{:S(2)}) copy-start(f32[160,512]{1,0:T(8,128)} %fusion.102) | copy-start | bytes 983044
  169.4 7.8 %copy-start.6 = (f32[4,160,160]{1,2,0:T(8,128)S(1)}, f32[4,160,160]{1,2,0:T(8,128)}, u32[]{:S(2)}) copy-start(f32[4,160,160]{1,2,0:T(8,128)} %fusion.28) | copy-start | bytes 1228804
  169.4 225.9 %reduce-scatter.7.cloned.1.call-start = ((), (), s32[]{:S(2)}) async-start(), calls=%async_computation.4 | async-start | bytes 7864320 | tf_op jit(solution)/shard_map/reduce_scatter | solution.py:116
  175.4 0.7 copy-start.10
  185.5 323.8 %reduce-scatter.9.cloned.1.call-start = ((), (), s32[]{:S(2)}) async-start(), calls=%async_computation.5 | async-start | bytes 7864320 | tf_op jit(solution)/shard_map/reduce_scatter | solution.py:119
  193.5 0.9 copy-start.11
  193.6 429.8 %reduce-scatter.11.cloned.1.call-start = ((), (), s32[]{:S(2)}) async-start(), calls=%async_computation.6 | async-start | bytes 7864320 | tf_op jit(solution)/shard_map/reduce_scatter | solution.py:122
  199.1 1.1 copy-start.3
  199.1 1.1 copy-start.16
  199.1 1.1 copy-start.17
  199.2 424.2 %copy-start.1 = (bf16[1,128,6144]{2,1,0:T(8,128)(2,1)S(1)}, bf16[1,128,6144]{2,1,0:T(8,128)(2,1)}, u32[]{:S(2)}) copy-start(bf16[1,128,6144]{2,1,0:T(8,128)(2,1)} %param.10) | copy-start | bytes 4718596
Sparse Core Ops, SparseCore 0:
  11.6 31.7 all-gather.4
  129.2 30.0 all-gather.6
  169.5 111.7 reduce-scatter.12
  284.1 111.2 reduce-scatter.6
  398.0 111.2 reduce-scatter.8
  512.1 111.2 reduce-scatter.10
where the time goes:
time: 632 us; the launch traced here: 630 us
  waiting for transfers between devices  416 us (66%)
  blocking collectives  92.5 us (15%)
  matrix products  66.3 us (10%)
  local copies, waits for them, and re-layouts  27.4 us (4%)
  between operations  16.4 us (3%)
    reduce_scatter x1, waiting for transfers between devices, body(): lax.psum_scatter(value_term.astype(jnp.bfloat16), 'dp', scatter_dimension...  114 us
    reduce_scatter x1, waiting for transfers between devices, body(): lax.psum_scatter(key_term.astype(jnp.bfloat16), 'dp', scatter_dimension=0...  114 us
    reduce_scatter x1, waiting for transfers between devices, body(): lax.psum_scatter(query_term.astype(jnp.bfloat16), 'dp', scatter_dimension...  114 us
    psum x1, blocking collectives, body(): grad_router = lax.psum(router_part, ('dp', 'ctx'))  47 us
    unnamed x2, blocking collectives  45.5 us
    all_gather x1, waiting for transfers between devices, body(): lax.all_gather(delta, 'ctx', axis=0, tiled=True)  30.2 us
    reduce_scatter x1, waiting for transfers between devices, body(): lax.psum_scatter(out_term.astype(jnp.bfloat16), 'dp', scatter_dimension=1...  29.3 us
    unnamed x49, local copies, waits for them, and re-layouts  21.9 us
  transfers between devices with their start and end apart: 8, of which 6 were waited for; matrix products, arithmetic and copies ran while one was open for 6% of the time, Pallas kernels for 0%

commit v1 on v0

--- a/solution.py
+++ b/solution.py
@@ -8,6 +8,27 @@
 HIGHEST_PRECISION = lax.Precision.HIGHEST
 ROW_CONTRACT = (((0,), (0,)), ((), ()))
 COLUMN_CONTRACT = (((1,), (1,)), ((), ()))
+
+
+def gather_around(x, axis, dim):
+    size, index, width = (lax.axis_size(axis), lax.axis_index(axis), x.shape[dim])
+    right = [(i, (i + 1) % size) for i in range(size)]
+    behind = [(i, (i - 1) % size) for i in range(size)]
+    result = jnp.zeros((*x.shape[:dim], size * width, *x.shape[dim + 1 :]), x.dtype)
+    result = lax.dynamic_update_slice_in_dim(result, x, index * width, axis=dim)
+    from_left = from_right = x
+    halfway = size // 2
+    for step in range(1, halfway + 1):
+        from_left = lax.ppermute(from_left, axis, right)
+        result = lax.dynamic_update_slice_in_dim(
+            result, from_left, (index - step) % size * width, axis=dim
+        )
+        if step < size - halfway:
+            from_right = lax.ppermute(from_right, axis, behind)
+            result = lax.dynamic_update_slice_in_dim(
+                result, from_right, (index + step) % size * width, axis=dim
+            )
+    return result
 
 
 def head_norm(values, width):
@@ -45,7 +66,7 @@
     )
     delta = (weights[:, None] * rows_back).astype(jnp.bfloat16)
     all_normed, all_delta, all_present = (
-        lax.all_gather(normed, "ctx", axis=0, tiled=True),
+        gather_around(normed, "ctx", 0),
         lax.all_gather(delta, "ctx", axis=0, tiled=True),
         lax.all_gather(present.astype(jnp.bfloat16), "ctx", axis=0, tiled=True),
     )

time: 632 us -> 653 us (1.033)
  local copies, waits for them, and re-layouts: 27.4 us -> 44 us
  starting transfers between devices: 5.63 us -> 13.7 us
    dynamic_update_slice x0 -> x8, local copies, waits for them, and re-layouts: none -> 18.1 us  [the longest x4 8.95 us: gather_around(): lax.dynamic_update_slice_in_dim(result, from_left, (index - step) % size...]
    all_gather x1 -> x0, waiting for transfers between devices: 14.3 us -> none  [body(): lax.all_gather(normed, 'ctx', axis=0, tiled=True)]
    ppermute x0 -> x7, waiting for transfers between devices: none -> 8.96 us  [the longest x4 7.44 us: gather_around(): from_left = lax.ppermute(from_left, axis, right)]
    ppermute x0 -> x7, starting transfers between devices: none -> 7.19 us  [the longest x3 6.19 us: gather_around(): from_right = lax.ppermute(from_right, axis, behind)]
    unnamed x49 -> x56, local copies, waits for them, and re-layouts: 21.9 us -> 20.2 us
  transfers between devices with their start and end apart: 8 -> 14, of which waited for: 6 -> 8; matrix products, arithmetic and copies ran while one was open for 6% -> 8% of each run, Pallas kernels for 0% -> 0%
where the time goes in v1:
time: 653 us; the launch traced here: 651 us
  waiting for transfers between devices  410 us (63%)
  blocking collectives  95.7 us (15%)
  matrix products  66.2 us (10%)
  local copies, waits for them, and re-layouts  44 us (7%)
  between operations  16.2 us (2%)
  starting transfers between devices  13.7 us (2%)
    reduce_scatter x1, waiting for transfers between devices, body(): lax.psum_scatter(query_term.astype(jnp.bfloat16), 'dp', scatter_dimension...  114 us
    reduce_scatter x1, waiting for transfers between devices, body(): lax.psum_scatter(key_term.astype(jnp.bfloat16), 'dp', scatter_dimension=0...  114 us
    reduce_scatter x1, waiting for transfers between devices, body(): lax.psum_scatter(value_term.astype(jnp.bfloat16), 'dp', scatter_dimension...  114 us
    unnamed x2, blocking collectives  48.4 us
    psum x1, blocking collectives, body(): grad_router = lax.psum(router_part, ('dp', 'ctx'))  47.3 us
    all_gather x1, waiting for transfers between devices, body(): lax.all_gather(delta, 'ctx', axis=0, tiled=True)  29.9 us
    reduce_scatter x1, waiting for transfers between devices, body(): lax.psum_scatter(out_term.astype(jnp.bfloat16), 'dp', scatter_dimension=1...  29.3 us
    unnamed x56, local copies, waits for them, and re-layouts  20.2 us
  transfers between devices with their start and end apart: 14, of which 8 were waited for; matrix products, arithmetic and copies ran while one was open for 8% of the time, Pallas kernels for 0%

profile of v1, /device:TPU:0, one launch (start us, length us, event | category | flops | bytes accessed | tf_op | source)
XLA Modules:
  0.0 651.4 jit_solution(1911106701060380562)
XLA Ops:
  8.7 1.9 multiply_reduce_fusion.1
  12.2 3.3 collective-permute-start.1
  15.5 4.2 collective-permute-done
  19.8 1.5 collective-permute-done.1
  21.3 2.8 collective-permute-start.3
  24.1 3.2 collective-permute-done.2
  28.8 16.9 %all-reduce = bf16[160]{0:T(256)(128)(2,1)S(1)} all-reduce(bf16[160]{0:T(256)(128)(2,1)S(1)} %dynamic-update-slice), channel_id=1, replica_groups=mesh['dp'=4,'ctx'=8] {'ctx'}, use_global_device_ids=true, to_apply=%add | all-reduce | flops 160 | bytes 640
  46.5 2.3 dynamic_update_slice.24
  49.5 2.1 dynamic_update_slice.25
  51.6 2.3 dynamic_update_slice.26
  53.9 2.3 dynamic_update_slice.27
  56.2 2.3 dynamic_update_slice.28
  58.5 2.3 dynamic_update_slice.29
  60.8 2.3 dynamic_update_slice.30
  63.1 2.3 dynamic_update_slice.31
  65.5 4.8 fusion.16
  70.2 4.8 fusion.102
  75.1 1.9 fusion.101
  77.0 1.8 reshape.116
  78.8 1.9 multiply_reduce_fusion.5
  81.7 1.8 reshape.117
  83.5 1.9 multiply_reduce_fusion.4
  86.3 2.4 fusion.28
  88.7 1.5 fusion.14
  90.8 5.3 convolution_convert_fusion.4
  96.2 31.4 %fusion = bf16[24,6144]{1,0:T(8,128)(2,1)} fusion(bf16[160,6144]{1,0:T(8,128)(2,1)} %convolution_convert_fusion.4), kind=kCustom, calls=%all-reduce-scatter | all-reduce-scatter fusion | flops 1179649 | bytes 2261504
  127.6 2.0 collective-permute-start.7
  129.6 1.5 slice
  131.2 4.1 collective-permute-start.8
  135.2 2.3 fusion.21
  138.2 9.5 %concatenate = bf16[52,6144]{1,0:T(8,128)(2,1)} concatenate(bf16[4,6144]{1,0:T(4,128)(2,1)} %collective-permute-done.8, bf16[24,6144]{1,0:T(8,128)(2,1)} %collective-permute-done.7, bf16[24,6144]{1,0:T(8,128)(2,1)} %fusion), dimensions={0} | concatenate | bytes 1277952
  147.7 2.7 fusion.26
  150.7 29.9 %all-gather.3.cloned.1.call-done = bf16[8,20,6144]{2,1,0:T(8,128)(2,1)} async-done(((bf16[1,20,6144]{2,1,0:T(8,128)(2,1)}), bf16[8,20,6144]{2,1,0:T(8,128)(2,1)}) %all-gather.3.cloned.1.call-update) | async-done | bytes 1966096 | tf_op jit(solution)/shard_map/all_gather | solution.py:70
  180.5 4.0 reshape.127
  184.6 6.1 convolution_convert_fusion
  190.7 5.7 fusion.17
  197.1 1.1 fusion.47
  198.2 2.6 multiply_reduce_fusion.3
  200.8 5.6 convolution_convert_fusion.3
  206.6 2.4 multiply_reduce_fusion.2
  209.0 5.6 convolution_convert_fusion.2
  215.7 4.4 convolution_convert_fusion.1
  221.6 47.3 %psum.7 = f32[6144]{0:T(1024)} all-reduce(f32[6144]{0:T(1024)S(1)} %bitcast.167), channel_id=1, replica_groups=mesh['dp'=4,'ctx'=8] {'dp','ctx'}, use_global_device_ids=true, to_apply=%region_13.14 | all-reduce | flops 6144 | bytes 49152 | tf_op jit(solution)/shard_map/psum | solution.py:104
  268.9 4.4 fusion.3
  273.3 29.3 %reduce-scatter.13.cloned.1.call-done = bf16[512,1536]{1,0:T(8,128)(2,1)} async-done(((bf16[512,6144]{1,0:T(8,128)(2,1)}), bf16[512,1536]{1,0:T(8,128)(2,1)}) %reduce-scatter.13.cloned.1.call-update) | async-done | bytes 1572880 | tf_op jit(solution)/shard_map/reduce_scatter | solution.py:146
  302.6 114.2 %reduce-scatter.7.cloned.1.call-done = bf16[1536,512]{1,0:T(8,128)(2,1)} async-done(((bf16[6144,512]{1,0:T(8,128)(2,1)}), bf16[1536,512]{1,0:T(8,128)(2,1)}) %reduce-scatter.7.cloned.1.call-update) | async-done | bytes 1572880 | tf_op jit(solution)/shard_map/reduce_scatter | solution.py:137
  416.8 114.0 %reduce-scatter.9.cloned.1.call-done = bf16[1536,512]{1,0:T(8,128)(2,1)} async-done(((bf16[6144,512]{1,0:T(8,128)(2,1)}), bf16[1536,512]{1,0:T(8,128)(2,1)}) %reduce-scatter.9.cloned.1.call-update) | async-done | bytes 1572880 | tf_op jit(solution)/shard_map/reduce_scatter | solution.py:140
  530.8 114.0 %reduce-scatter.11.cloned.1.call-done = bf16[1536,512]{1,0:T(8,128)(2,1)} async-done(((bf16[6144,512]{1,0:T(8,128)(2,1)}), bf16[1536,512]{1,0:T(8,128)(2,1)}) %reduce-scatter.11.cloned.1.call-update) | async-done | bytes 1572880 | tf_op jit(solution)/shard_map/reduce_scatter | solution.py:143
  (88 shorter events, 10.9 us)
Async XLA Ops:
  7.2 140.5 %copy-start = (bf16[1,128,6144]{2,1,0:T(8,128)(2,1)S(1)}, bf16[1,128,6144]{2,1,0:T(8,128)(2,1)}, u32[]{:S(2)}) copy-start(bf16[1,128,6144]{2,1,0:T(8,128)(2,1)} %param.10) | copy-start | bytes 4718596
  7.2 20.1 %copy-start.22 = (u32[32]{0:T(128)S(1)}, u32[32]{0:T(128)}, u32[]{:S(2)}) copy-start(u32[32]{0:T(128)} %constant.94) | copy-start | bytes 388
  7.2 173.3 %all-gather.3.cloned.1.call-start = ((), (), s32[]{:S(2)}) async-start(), calls=%async_computation.8 | async-start | bytes 2654208 | tf_op jit(solution)/shard_map/all_gather | solution.py:70
  8.7 1.9 copy-start.16
  8.7 1.9 copy-start.18
  10.6 0.8 copy-start.2
  11.5 0.7 copy-start.12
  11.5 8.3 %collective-permute-start = (bf16[20,6144]{1,0:T(8,128)(2,1)S(1)}, bf16[20,6144]{1,0:T(8,128)(2,1)S(1)}, u32[]{:S(2)}, u32[]{:S(2)}) collective-permute-start(bf16[20,6144]{1,0:T(8,128)(2,1)S(1)} %multiply_convert_fusion.1), channel_id=1, source_target_pairs={{0,1},{1,2},{2,3},{3,4},{4,5},{5,6},{6,7},{7,0},{8,9},{9,10},{10,1... | collective-permute-start | bytes 737288 | tf_op jit(solution)/shard_map/ppermute | solution.py:22
  12.2 9.1 %collective-permute-start.1 = (bf16[20,6144]{1,0:T(8,128)(2,1)S(1)}, bf16[20,6144]{1,0:T(8,128)(2,1)S(1)}, u32[]{:S(2)}, u32[]{:S(2)}) collective-permute-start(bf16[20,6144]{1,0:T(8,128)(2,1)S(1)} %multiply_convert_fusion.1), channel_id=1, source_target_pairs={{0,7},{1,0},{2,1},{3,2},{4,3},{5,4},{6,5},{7,6},{8,15},{9,8},{10,9... | collective-permute-start | bytes 737288 | tf_op jit(solution)/shard_map/ppermute | solution.py:27
  19.8 1.5 copy-start.13
  19.8 7.5 %collective-permute-start.2 = (bf16[20,6144]{1,0:T(8,128)(2,1)S(1)}, bf16[20,6144]{1,0:T(8,128)(2,1)S(1)}, u32[]{:S(2)}, u32[]{:S(2)}) collective-permute-start(bf16[20,6144]{1,0:T(8,128)(2,1)S(1)} %collective-permute-done), channel_id=1, source_target_pairs={{0,1},{1,2},{2,3},{3,4},{4,5},{5,6},{6,7},{7,0},{8,9},{9,10},{10,1... | collective-permute-start | bytes 737288 | tf_op jit(solution)/shard_map/ppermute | solution.py:22
  21.3 25.0 %copy-start.14 = (bf16[20,6144]{1,0:T(8,128)(2,1)}, bf16[20,6144]{1,0:T(8,128)(2,1)S(1)}, u32[]{:S(2)}) copy-start(bf16[20,6144]{1,0:T(8,128)(2,1)S(1)} %collective-permute-done.1) | copy-start | bytes 737284
  21.3 24.4 %collective-permute-start.3 = (bf16[20,6144]{1,0:T(8,128)(2,1)S(1)}, bf16[20,6144]{1,0:T(8,128)(2,1)}, u32[]{:S(2)}, u32[]{:S(2)}) collective-permute-start(bf16[20,6144]{1,0:T(8,128)(2,1)S(1)} %collective-permute-done.1), channel_id=1, source_target_pairs={{0,7},{1,0},{2,1},{3,2},{4,3},{5,4},{6,5},{7,6},{8,15},{9,8},{10,9... | collective-permute-start | bytes 737288 | tf_op jit(solution)/shard_map/ppermute | solution.py:27
  27.3 19.0 %copy-start.15 = (bf16[20,6144]{1,0:T(8,128)(2,1)}, bf16[20,6144]{1,0:T(8,128)(2,1)S(1)}, u32[]{:S(2)}) copy-start(bf16[20,6144]{1,0:T(8,128)(2,1)S(1)} %collective-permute-done.2) | copy-start | bytes 737284
  27.3 18.5 %collective-permute-start.4 = (bf16[20,6144]{1,0:T(8,128)(2,1)S(1)}, bf16[20,6144]{1,0:T(8,128)(2,1)}, u32[]{:S(2)}, u32[]{:S(2)}) collective-permute-start(bf16[20,6144]{1,0:T(8,128)(2,1)S(1)} %collective-permute-done.2), channel_id=1, source_target_pairs={{0,1},{1,2},{2,3},{3,4},{4,5},{5,6},{6,7},{7,0},{8,9},{9,10},{10,1... | collective-permute-start | bytes 737288 | tf_op jit(solution)/shard_map/ppermute | solution.py:22
  45.8 15.1 %collective-permute-start.5 = (bf16[20,6144]{1,0:T(8,128)(2,1)}, bf16[20,6144]{1,0:T(8,128)(2,1)}, u32[]{:S(2)}, u32[]{:S(2)}) collective-permute-start(bf16[20,6144]{1,0:T(8,128)(2,1)} %collective-permute-done.3), channel_id=1, source_target_pairs={{0,7},{1,0},{2,1},{3,2},{4,3},{5,4},{6,5},{7,6},{8,15},{9,8},{10,9... | collective-permute-start | bytes 737288 | tf_op jit(solution)/shard_map/ppermute | solution.py:27
  45.8 17.3 %collective-permute-start.6 = (bf16[20,6144]{1,0:T(8,128)(2,1)}, bf16[20,6144]{1,0:T(8,128)(2,1)}, u32[]{:S(2)}, u32[]{:S(2)}) collective-permute-start(bf16[20,6144]{1,0:T(8,128)(2,1)} %collective-permute-done.4), channel_id=1, source_target_pairs={{0,1},{1,2},{2,3},{3,4},{4,5},{5,6},{6,7},{7,0},{8,9},{9,10},{10,1... | collective-permute-start | bytes 737288 | tf_op jit(solution)/shard_map/ppermute | solution.py:22
  65.4 9.6 %slice-start = ((s8[6291456]{0:T(1024)(128)(4,1)}), s8[4194304]{0:T(1024)(128)(4,1)S(1)}, s32[]{:S(2)}) async-start(s8[6291456]{0:T(1024)(128)(4,1)} %bitcast.165), calls=%async_computation.9 | async-start | bytes 8388608
  70.2 4.8 slice-start.1
  90.2 0.7 copy-start.7
  96.2 51.5 %copy-start.17 = (pred[20]{0:T(512)(128)(4,1)S(1)}, pred[20]{0:T(512)(128)(4,1)}, u32[]{:S(2)}) copy-start(pred[20]{0:T(512)(128)(4,1)} %copy-done.16) | copy-start | bytes 64
  96.2 51.5 %copy-start.19 = (s32[20]{0:T(128)S(1)}, s32[20]{0:T(128)}, u32[]{:S(2)}) copy-start(s32[20]{0:T(128)} %copy-done.18) | copy-start | bytes 244
  127.6 10.5 %collective-permute-start.7 = (bf16[24,6144]{1,0:T(8,128)(2,1)}, bf16[24,6144]{1,0:T(8,128)(2,1)}, u32[]{:S(2)}, u32[]{:S(2)}) collective-permute-start(bf16[24,6144]{1,0:T(8,128)(2,1)} %fusion), channel_id=1, source_target_pairs={{0,1},{1,2},{2,3},{3,4},{4,5},{5,6},{6,7},{8,9},{9,10},{10,11},{11... | collective-permute-start | bytes 884744
  131.2 7.0 %collective-permute-start.8 = (bf16[4,6144]{1,0:T(4,128)(2,1)}, bf16[4,6144]{1,0:T(4,128)(2,1)}, u32[]{:S(2)}, u32[]{:S(2)}) collective-permute-start(bf16[4,6144]{1,0:T(4,128)(2,1)} %slice), channel_id=1, source_target_pairs={{0,2},{1,3},{2,4},{3,5},{4,6},{5,7},{8,10},{9,11},{10,12},{11,13},... | collective-permute-start | bytes 147464
  150.4 34.1 %copy-start.8 = (bf16[4,20,8,128]{3,2,1,0:T(8,128)(2,1)S(1)}, bf16[4,20,8,128]{3,2,1,0:T(8,128)(2,1)}, u32[]{:S(2)}) copy-start(bf16[4,20,8,128]{3,2,1,0:T(8,128)(2,1)} %copy-done.7) | copy-start | bytes 491524
  150.4 152.2 %reduce-scatter.13.cloned.1.call-start = ((), (), s32[]{:S(2)}) async-start(), calls=%async_computation.7 | async-start | bytes 7864320 | tf_op jit(solution)/shard_map/reduce_scatter | solution.py:146
  190.6 6.5 copy-start.9
  190.7 7.6 %copy-start.4 = (f32[160,512]{1,0:T(8,128)S(1)}, f32[160,512]{1,0:T(8,128)}, u32[]{:S(2)}) copy-start(f32[160,512]{1,0:T(8,128)} %fusion.102) | copy-start | bytes 983044
  190.7 7.5 %copy-start.5 = (f32[160,512]{1,0:T(8,128)S(1)}, f32[160,512]{1,0:T(8,128)}, u32[]{:S(2)}) copy-start(f32[160,512]{1,0:T(8,128)} %fusion.101) | copy-start | bytes 983044
  190.7 7.5 %copy-start.6 = (f32[4,160,160]{1,2,0:T(8,128)S(1)}, f32[4,160,160]{1,2,0:T(8,128)}, u32[]{:S(2)}) copy-start(f32[4,160,160]{1,2,0:T(8,128)} %fusion.28) | copy-start | bytes 1228804
  190.7 226.1 %reduce-scatter.7.cloned.1.call-start = ((), (), s32[]{:S(2)}) async-start(), calls=%async_computation.4 | async-start | bytes 7864320 | tf_op jit(solution)/shard_map/reduce_scatter | solution.py:137
  196.5 0.7 copy-start.10
  206.5 324.3 %reduce-scatter.9.cloned.1.call-start = ((), (), s32[]{:S(2)}) async-start(), calls=%async_computation.5 | async-start | bytes 7864320 | tf_op jit(solution)/shard_map/reduce_scatter | solution.py:140
  214.6 0.9 copy-start.11
  214.6 430.3 %reduce-scatter.11.cloned.1.call-start = ((), (), s32[]{:S(2)}) async-start(), calls=%async_computation.6 | async-start | bytes 7864320 | tf_op jit(solution)/shard_map/reduce_scatter | solution.py:143
  220.1 1.1 copy-start.3
  220.1 1.1 copy-start.20
  220.1 1.1 copy-start.21
  220.2 424.7 %copy-start.1 = (bf16[1,128,6144]{2,1,0:T(8,128)(2,1)S(1)}, bf16[1,128,6144]{2,1,0:T(8,128)(2,1)}, u32[]{:S(2)}) copy-start(bf16[1,128,6144]{2,1,0:T(8,128)(2,1)} %param.10) | copy-start | bytes 4718596
Sparse Core Ops, SparseCore 0:
  150.6 29.9 all-gather.2
  190.8 111.7 reduce-scatter.12
  305.5 111.2 reduce-scatter.6
  419.5 111.2 reduce-scatter.8
  533.6 111.2 reduce-scatter.10
